TPU v7x, 32 devices: a whole 2x2x4 slice. The times are simulated.
32 devices in a mesh: blk: 8 (over z, core), help: 4 (over y, x).
Axes of the slice: x: 2, y: 2, z: 4, core: 2. Of those that a mesh axis runs over, the one named last changes fastest.
Arguments:
- vectors: float32 [8, 16384], P(None, ('blk', 'help')), may hold values from -6 to 6
- tile_blocks: float32 [32, 5, 3, 256, 256], P(('blk', 'help')), may hold values from -0.1875 to 0.1875
- tile_row: int32 [32, 5, 3], P(('blk', 'help')), may hold values from 0 to 7
- tile_col: int32 [32, 5, 3], P(('blk', 'help')), may hold values from 0 to 7
- counts: int32 [32, 5], P(('blk', 'help')), may hold values from 1 to 3, as said below
Outputs:
- product: float32 [8, 16384], P(None, ('blk', 'help'))
- gram_energy: float32 [8, 8], replicated
- gram_correlation: float32 [8, 8], replicated
Inputs may be any that keep to these rules, and one draw needn't show every extreme that they name: `counts`: in every group of 4 helpers one helper has 3 live slots for every band offset; every other helper has fewer, and at least one, for each offset.
All inputs are finite; a program needn't handle non-finite values.
Results may differ from a plain program's by a relative error of at most 0.0003.
Values sent between devices are 32-bit elements; how exact they have to be, the bound alone decides.
No kernel may reach another device: no remote copies, remote signals or barrier semaphores. Data moves between devices by JAX's collectives and lax.ppermute only.
A program may use at most 64 MiB of HBM per device.

v0:
```python
import jax
import jax.numpy as jnp
from jax import lax
from jax.sharding import PartitionSpec as P

VEC = 8
TILE = 256
BAND = 2
SLOTS = 3
NOFF = 5


def shifted(value, axis, steps):
    count = lax.axis_size(axis)
    initial, last = (max(0, -steps), min(count, count - steps))
    return lax.ppermute(value, axis, [(source, source + steps) for source in range(initial, last)])


def neighbour_panels(source):
    lowers = []
    uppers = []
    current = source
    for hop_index in range(BAND):
        current = shifted(current, "blk", 1)
        lowers.append(current)
    current = source
    for hop_index in range(BAND):
        current = shifted(current, "blk", -1)
        uppers.append(current)
    return lowers[::-1] + [source] + uppers


def local(vectors, tile_blocks, tile_row, tile_col, counts):
    groups = lax.axis_size("blk")
    piece_width = vectors.shape[1]
    group_width = piece_width * lax.axis_size("help")
    group_rows = group_width // TILE
    full_panel = lax.all_gather(vectors, "help", axis=1, tiled=True)
    panels = neighbour_panels(full_panel)
    slot_ids = jnp.arange(SLOTS, dtype=jnp.int32)
    row_ids = jnp.arange(group_rows, dtype=jnp.int32)
    partial_value = jnp.zeros((VEC, group_rows, TILE), jnp.float32)
    for offset_index in range(NOFF):
        panel_tiles = panels[offset_index].reshape(VEC, group_rows, TILE)
        pieces = jnp.take(panel_tiles, tile_col[0, offset_index], axis=1)
        live = (slot_ids < counts[0, offset_index]).astype(jnp.float32)
        contribution = jnp.einsum(
            "ist,stu->isu", pieces, tile_blocks[0, offset_index], precision=lax.Precision.HIGHEST
        )
        one_hot = (tile_row[0, offset_index][:, None] == row_ids[None, :]).astype(
            jnp.float32
        ) * live[:, None]
        partial_value = partial_value + jnp.einsum(
            "isu,sr->iru", contribution, one_hot, precision=lax.Precision.HIGHEST
        )
    flattened = partial_value.reshape(VEC, group_width)
    basis_size = float(groups * group_width)
    correlation_term = jnp.dot(
        vectors, vectors.T, precision=lax.Precision.HIGHEST, preferred_element_type=jnp.float32
    )
    own_panel = panels[BAND]
    early_terms = (
        jnp.dot(
            own_panel,
            flattened.T,
            precision=lax.Precision.HIGHEST,
            preferred_element_type=jnp.float32,
        ),
        correlation_term,
    )
    gram_energy, gram_correlation = lax.psum((early_terms[0], early_terms[1]), ("blk", "help"))
    product = lax.psum_scatter(flattened, "help", scatter_dimension=1, tiled=True)
    return (product, gram_energy / basis_size, gram_correlation / basis_size)


def solution(mesh):
    placed = (
        P(None, ("blk", "help")),
        P(("blk", "help"), None, None, None, None),
        P(("blk", "help"), None, None),
        P(("blk", "help"), None, None),
        P(("blk", "help"), None),
    )
    return jax.shard_map(
        local,
        mesh=mesh,
        in_specs=placed,
        out_specs=(P(None, ("blk", "help")), P(), P()),
        check_vma=False,
    )
```

profile of v0, /device:TPU:0, one launch (start us, length us, event | category | flops | bytes accessed | tf_op | source)
XLA Modules:
  0.0 99.4 jit_solution(237913537589706720)
XLA Ops:
  7.2 9.8 %all_gather.3 = f32[8,2048]{1,0:T(8,128)S(1)} all-gather(f32[8,512]{1,0:T(8,128)} %param.7), channel_id=1, replica_groups=mesh['blk'=8,'help'=4] {'help'}, dimensions={1}, use_global_device_ids=true | all-gather | bytes 81920 | tf_op jit(solution)/shard_map/all_gather | solution.py:38
  17.1 1.3 %collective-permute-start = (f32[8,2048]{1,0:T(8,128)S(1)}, f32[8,2048]{1,0:T(8,128)S(1)}, u32[]{:S(2)}, u32[]{:S(2)}) collective-permute-start(f32[8,2048]{1,0:T(8,128)S(1)} %all_gather.3), channel_id=1, source_target_pairs={{0,4},{4,8},{8,12},{12,16},{16,20},{20,24},{24,28},{1,5},{5,9},{9,... | collective-permute-start | bytes 196616 | tf_op jit(solution)/shard_map/ppermute | solution.py:16
  18.3 1.3 %collective-permute-start.2 = (f32[8,2048]{1,0:T(8,128)S(1)}, f32[8,2048]{1,0:T(8,128)S(1)}, u32[]{:S(2)}, u32[]{:S(2)}) collective-permute-start(f32[8,2048]{1,0:T(8,128)S(1)} %all_gather.3), channel_id=1, source_target_pairs={{4,0},{8,4},{12,8},{16,12},{20,16},{24,20},{28,24},{5,1},{9,5},{13... | collective-permute-start | bytes 196616 | tf_op jit(solution)/shard_map/ppermute | solution.py:16
  19.6 1.3 %slice_reduce_fusion = (s32[3]{0:T(128)S(1)}, s32[3]{0:T(128)S(1)}, s32[3]{0:T(128)S(1)}, s32[3]{0:T(128)S(1)}, s32[3]{0:T(128)S(1)}) fusion(s32[1,5,3]{1,0,2:T(1,128)} %param.10), kind=kLoop, calls=%fused_computation.94 | loop fusion | bytes 120 | tf_op jit(solution)/shard_map/slice | solution.py:45
  21.1 0.9 fusion.83
  22.0 1.4 %fusion.82 = (s32[1,1]{1,0:T(1,128)}, s32[1,1]{1,0:T(1,128)}, s32[1,1]{1,0:T(1,128)}, s32[1,1]{1,0:T(1,128)}, s32[1,1]{1,0:T(1,128)}) fusion(s32[1,5]{1,0:T(1,128)} %param.11), kind=kLoop, calls=%fused_computation.129 | loop fusion | bytes 40 | tf_op jit(solution)/shard_map/slice | solution.py:46
  23.5 0.7 compare_convert_fusion.4
  24.2 1.3 %slice_reduce_fusion.1 = (s32[3]{0:T(128)S(1)}, s32[3]{0:T(128)S(1)}, s32[3]{0:T(128)S(1)}, s32[3]{0:T(128)S(1)}, s32[3]{0:T(128)S(1)}) fusion(s32[1,5,3]{1,0,2:T(1,128)} %param.9), kind=kLoop, calls=%fused_computation.95 | loop fusion | bytes 120 | tf_op jit(solution)/shard_map/slice | solution.py:50
  25.5 0.7 compare_convert_fusion.3
  26.2 0.7 compare_convert_fusion.2
  28.0 1.6 %fusion.5 = f32[3,8,256]{2,1,0:T(8,128)S(1)} fusion(f32[1,5,3,256,256]{4,3,2,1,0:T(8,128)} %param.8, f32[3,8,256]{2,1,0:T(8,128)S(1)} %gather_fusion.2, pred[3]{0:T(512)(128)(4,1)S(1)} %compare_and_fusion.2), kind=kOutput, calls=%fused_computation.15 | convolution fusion | flops 18880512 | bytes 835587 | tf_op jit(solution)/shard_map/ist,stu->isu/dot_general | solution.py:47
  29.6 0.7 compare_convert_fusion
  30.8 1.6 %fusion.7 = f32[3,8,256]{2,1,0:T(8,128)S(1)} fusion(f32[1,5,3,256,256]{4,3,2,1,0:T(8,128)} %param.8, f32[3,8,256]{2,1,0:T(8,128)S(1)} %gather_fusion.1, pred[3]{0:T(512)(128)(4,1)S(1)} %compare_and_fusion.3), kind=kOutput, calls=%fused_computation.17 | convolution fusion | flops 18880512 | bytes 835587 | tf_op jit(solution)/shard_map/ist,stu->isu/dot_general | solution.py:47
  33.0 4.8 %collective-permute-start.1 = (f32[8,2048]{1,0:T(8,128)S(1)}, f32[8,2048]{1,0:T(8,128)S(1)}, u32[]{:S(2)}, u32[]{:S(2)}) collective-permute-start(f32[8,2048]{1,0:T(8,128)S(1)} %collective-permute-done), channel_id=1, source_target_pairs={{0,4},{4,8},{8,12},{12,16},{16,20},{20,24},{24,28},{1,5},{5,9},{9,... | collective-permute-start | bytes 196616 | tf_op jit(solution)/shard_map/ppermute | solution.py:16
  37.8 1.6 %fusion.3 = f32[3,8,256]{2,1,0:T(8,128)S(1)} fusion(f32[1,5,3,256,256]{4,3,2,1,0:T(8,128)} %param.8, f32[3,8,256]{2,1,0:T(8,128)S(1)} %gather_fusion.3, pred[3]{0:T(512)(128)(4,1)S(1)} %compare_and_fusion.1), kind=kOutput, calls=%fused_computation.13 | convolution fusion | flops 18880512 | bytes 835587 | tf_op jit(solution)/shard_map/ist,stu->isu/dot_general | solution.py:47
  39.4 1.3 %collective-permute-start.3 = (f32[8,2048]{1,0:T(8,128)S(1)}, f32[8,2048]{1,0:T(8,128)S(1)}, u32[]{:S(2)}, u32[]{:S(2)}) collective-permute-start(f32[8,2048]{1,0:T(8,128)S(1)} %collective-permute-done.2), channel_id=1, source_target_pairs={{4,0},{8,4},{12,8},{16,12},{20,16},{24,20},{28,24},{5,1},{9,5},{13... | collective-permute-start | bytes 196616 | tf_op jit(solution)/shard_map/ppermute | solution.py:16
  41.3 1.6 %fusion.9 = f32[3,8,256]{2,1,0:T(8,128)S(1)} fusion(f32[1,5,3,256,256]{4,3,2,1,0:T(8,128)} %param.8, f32[3,8,256]{2,1,0:T(8,128)S(1)} %gather_fusion, pred[3]{0:T(512)(128)(4,1)S(1)} %compare_and_fusion.4), kind=kOutput, calls=%fused_computation.19 | convolution fusion | flops 18880512 | bytes 835587 | tf_op jit(solution)/shard_map/ist,stu->isu/dot_general | solution.py:47
  42.9 0.9 collective-permute-done.3
  44.4 1.6 %fusion.1 = f32[3,8,256]{2,1,0:T(8,128)S(1)} fusion(f32[1,5,3,256,256]{4,3,2,1,0:T(8,128)} %param.8, f32[3,8,256]{2,1,0:T(8,128)S(1)} %gather_fusion.4, pred[3]{0:T(512)(128)(4,1)S(1)} %compare_and_fusion), kind=kOutput, calls=%fused_computation.11 | convolution fusion | flops 18880512 | bytes 835587 | tf_op jit(solution)/shard_map/ist,stu->isu/dot_general | solution.py:47
  47.7 0.6 copy.20
  48.3 1.0 %convolution_bitcast_fusion = f32[8,8]{0,1:T(8,128)S(1)} fusion(f32[8,2048]{1,0:T(8,128)} %bitcast.81, f32[8,2048]{1,0:T(8,128)S(1)} %all_gather.3), kind=kOutput, calls=%fused_computation.10 | convolution fusion | flops 1572864 | bytes 131328 | tf_op jit(solution)/shard_map/dot_general | solution.py:63
  49.4 41.8 %all-reduce = (f32[8,8]{0,1:T(8,128)S(1)}, f32[8,8]{0,1:T(8,128)S(1)}) all-reduce(f32[8,8]{0,1:T(8,128)S(1)} %convolution_bitcast_fusion, f32[8,8]{0,1:T(8,128)S(1)} %fusion.83), channel_id=1, replica_groups=mesh['blk'=8,'help'=4] {'blk','help'}, use_global_device_ids=true, to_apply=%region_1.3 | all-reduce | flops 128 | bytes 1024 | tf_op jit(solution)/shard_map/psum | solution.py:71
  91.2 0.7 copy.12
  91.9 0.7 copy.13
  (33 shorter events, 5.1 us)
Async XLA Ops:
  7.2 85.4 %reduce-scatter.2.cloned.1.call-start = ((), (), s32[]{:S(2)}) async-start(), calls=%async_computation.1 | async-start | bytes 81920 | tf_op jit(solution)/shard_map/reduce_scatter | solution.py:72
  17.1 13.2 %collective-permute-start = (f32[8,2048]{1,0:T(8,128)S(1)}, f32[8,2048]{1,0:T(8,128)S(1)}, u32[]{:S(2)}, u32[]{:S(2)}) collective-permute-start(f32[8,2048]{1,0:T(8,128)S(1)} %all_gather.3), channel_id=1, source_target_pairs={{0,4},{4,8},{8,12},{12,16},{16,20},{20,24},{24,28},{1,5},{5,9},{9,... | collective-permute-start | bytes 196616 | tf_op jit(solution)/shard_map/ppermute | solution.py:16
  18.3 14.1 %collective-permute-start.2 = (f32[8,2048]{1,0:T(8,128)S(1)}, f32[8,2048]{1,0:T(8,128)S(1)}, u32[]{:S(2)}, u32[]{:S(2)}) collective-permute-start(f32[8,2048]{1,0:T(8,128)S(1)} %all_gather.3), channel_id=1, source_target_pairs={{4,0},{8,4},{12,8},{16,12},{20,16},{24,20},{28,24},{5,1},{9,5},{13... | collective-permute-start | bytes 196616 | tf_op jit(solution)/shard_map/ppermute | solution.py:16
  33.0 7.8 %collective-permute-start.1 = (f32[8,2048]{1,0:T(8,128)S(1)}, f32[8,2048]{1,0:T(8,128)S(1)}, u32[]{:S(2)}, u32[]{:S(2)}) collective-permute-start(f32[8,2048]{1,0:T(8,128)S(1)} %collective-permute-done), channel_id=1, source_target_pairs={{0,4},{4,8},{8,12},{12,16},{16,20},{20,24},{24,28},{1,5},{5,9},{9,... | collective-permute-start | bytes 196616 | tf_op jit(solution)/shard_map/ppermute | solution.py:16
  39.4 4.4 %collective-permute-start.3 = (f32[8,2048]{1,0:T(8,128)S(1)}, f32[8,2048]{1,0:T(8,128)S(1)}, u32[]{:S(2)}, u32[]{:S(2)}) collective-permute-start(f32[8,2048]{1,0:T(8,128)S(1)} %collective-permute-done.2), channel_id=1, source_target_pairs={{4,0},{8,4},{12,8},{16,12},{20,16},{24,20},{28,24},{5,1},{9,5},{13... | collective-permute-start | bytes 196616 | tf_op jit(solution)/shard_map/ppermute | solution.py:16
Sparse Core Ops, SparseCore 0:
  48.5 25.5 reduce-scatter.1
where the time goes:
time: 100 us; the launch traced here: 99.4 us
  blocking collectives  51.7 us (52%)
  between operations  14.4 us (14%)
  matrix products  11.5 us (12%)
  starting transfers between devices  8.77 us (9%)
  local copies, waits for them, and re-layouts  8.77 us (9%)
  other arithmetic  3.34 us (3%)
    psum x1, blocking collectives, local(): lax.psum((early_terms[0], early_terms[1]), ('blk', 'help'))  41.8 us
    all_gather x1, blocking collectives, local(): full_panel = lax.all_gather(vectors, 'help', axis=1, tiled=True)  9.85 us
    ppermute x4, starting transfers between devices, shifted(): lax.ppermute(value, axis, [(source, source + steps) for source in range(i...  8.73 us
    dot_general x5, matrix products, local(): jnp.einsum('ist,stu->isu', pieces, tile_blocks[0, offset_index], precisio...  7.92 us
    convert_element_type x5, other arithmetic, local(): live = (slot_ids < counts[0, offset_index]).astype(jnp.float32)  3.23 us
    gather x5, local copies, waits for them, and re-layouts, local(): pieces = jnp.take(panel_tiles, tile_col[0, offset_index], axis=1)  2.77 us
  transfers between devices with their start and end apart: 5, of which 1 were waited for; matrix products, arithmetic and copies ran while one was open for 19% of the time, Pallas kernels for 0%

commit v1 on v0

--- a/solution.py
+++ b/solution.py
@@ -68,7 +68,9 @@
         ),
         correlation_term,
     )
-    gram_energy, gram_correlation = lax.psum((early_terms[0], early_terms[1]), ("blk", "help"))
+    gram_energy, gram_correlation = lax.psum(
+        lax.psum((early_terms[0], early_terms[1]), "help"), "blk"
+    )
     product = lax.psum_scatter(flattened, "help", scatter_dimension=1, tiled=True)
     return (product, gram_energy / basis_size, gram_correlation / basis_size)
 

time: 100 us -> 82.9 us (0.83)
  blocking collectives: 51.7 us -> 34.5 us
    psum x1 -> x2, blocking collectives: 41.8 us -> 24.6 us  [the longest x1 15.5 us: local(): lax.psum(lax.psum((early_terms[0], early_terms[1]), 'help'), 'blk')]
  transfers between devices with their start and end apart: 5 -> 5, of which waited for: 1 -> 1; matrix products, arithmetic and copies ran while one was open for 19% -> 23% of each run, Pallas kernels for 0% -> 0%
where the time goes in v1:
time: 82.9 us; the launch traced here: 82.2 us
  blocking collectives  34.5 us (42%)
  between operations  14.4 us (17%)
  matrix products  11.5 us (14%)
  starting transfers between devices  8.77 us (11%)
  local copies, waits for them, and re-layouts  8.77 us (11%)
  other arithmetic  3.34 us (4%)
  waiting for transfers between devices  0.95 us (1%)
    psum x1, blocking collectives, local(): lax.psum(lax.psum((early_terms[0], early_terms[1]), 'help'), 'blk')  15.5 us
    all_gather x1, blocking collectives, local(): full_panel = lax.all_gather(vectors, 'help', axis=1, tiled=True)  9.85 us
    psum x1, blocking collectives, local(): lax.psum((early_terms[0], early_terms[1]), 'help')  9.12 us
    ppermute x4, starting transfers between devices, shifted(): lax.ppermute(value, axis, [(source, source + steps) for source in range(i...  8.73 us
    dot_general x5, matrix products, local(): jnp.einsum('ist,stu->isu', pieces, tile_blocks[0, offset_index], precisio...  7.92 us
    convert_element_type x5, other arithmetic, local(): live = (slot_ids < counts[0, offset_index]).astype(jnp.float32)  3.23 us
    gather x5, local copies, waits for them, and re-layouts, local(): pieces = jnp.take(panel_tiles, tile_col[0, offset_index], axis=1)  2.77 us
    unnamed x3, local copies, waits for them, and re-layouts  1.96 us
  transfers between devices with their start and end apart: 5, of which 1 were waited for; matrix products, arithmetic and copies ran while one was open for 23% of the time, Pallas kernels for 0%

profile of v1, /device:TPU:0, one launch (start us, length us, event | category | flops | bytes accessed | tf_op | source)
XLA Modules:
  0.0 82.2 jit_solution(9111987876331550953)
XLA Ops:
  7.2 9.8 %all_gather.3 = f32[8,2048]{1,0:T(8,128)S(1)} all-gather(f32[8,512]{1,0:T(8,128)} %param.7), channel_id=1, replica_groups=mesh['blk'=8,'help'=4] {'help'}, dimensions={1}, use_global_device_ids=true | all-gather | bytes 81920 | tf_op jit(solution)/shard_map/all_gather | solution.py:38
  17.1 1.3 %collective-permute-start = (f32[8,2048]{1,0:T(8,128)S(1)}, f32[8,2048]{1,0:T(8,128)S(1)}, u32[]{:S(2)}, u32[]{:S(2)}) collective-permute-start(f32[8,2048]{1,0:T(8,128)S(1)} %all_gather.3), channel_id=1, source_target_pairs={{0,4},{4,8},{8,12},{12,16},{16,20},{20,24},{24,28},{1,5},{5,9},{9,... | collective-permute-start | bytes 196616 | tf_op jit(solution)/shard_map/ppermute | solution.py:16
  18.3 1.3 %collective-permute-start.2 = (f32[8,2048]{1,0:T(8,128)S(1)}, f32[8,2048]{1,0:T(8,128)S(1)}, u32[]{:S(2)}, u32[]{:S(2)}) collective-permute-start(f32[8,2048]{1,0:T(8,128)S(1)} %all_gather.3), channel_id=1, source_target_pairs={{4,0},{8,4},{12,8},{16,12},{20,16},{24,20},{28,24},{5,1},{9,5},{13... | collective-permute-start | bytes 196616 | tf_op jit(solution)/shard_map/ppermute | solution.py:16
  19.6 1.3 %slice_reduce_fusion = (s32[3]{0:T(128)S(1)}, s32[3]{0:T(128)S(1)}, s32[3]{0:T(128)S(1)}, s32[3]{0:T(128)S(1)}, s32[3]{0:T(128)S(1)}) fusion(s32[1,5,3]{1,0,2:T(1,128)} %param.10), kind=kLoop, calls=%fused_computation.94 | loop fusion | bytes 120 | tf_op jit(solution)/shard_map/slice | solution.py:45
  21.1 0.9 %fusion.83 = f32[8,8]{0,1:T(8,128)S(1)} fusion(f32[8,512]{1,0:T(8,128)} %param.7), kind=kOutput, calls=%fused_computation.130 | convolution fusion | flops 393216 | bytes 16640 | tf_op jit(solution)/shard_map/dot_general | solution.py:58
  22.0 1.4 %fusion.82 = (s32[1,1]{1,0:T(1,128)}, s32[1,1]{1,0:T(1,128)}, s32[1,1]{1,0:T(1,128)}, s32[1,1]{1,0:T(1,128)}, s32[1,1]{1,0:T(1,128)}) fusion(s32[1,5]{1,0:T(1,128)} %param.11), kind=kLoop, calls=%fused_computation.129 | loop fusion | bytes 40 | tf_op jit(solution)/shard_map/slice | solution.py:46
  23.5 0.7 compare_convert_fusion.4
  24.2 1.3 %slice_reduce_fusion.1 = (s32[3]{0:T(128)S(1)}, s32[3]{0:T(128)S(1)}, s32[3]{0:T(128)S(1)}, s32[3]{0:T(128)S(1)}, s32[3]{0:T(128)S(1)}) fusion(s32[1,5,3]{1,0,2:T(1,128)} %param.9), kind=kLoop, calls=%fused_computation.95 | loop fusion | bytes 120 | tf_op jit(solution)/shard_map/slice | solution.py:50
  25.5 0.7 compare_convert_fusion.3
  26.2 0.7 compare_convert_fusion.2
  28.0 1.6 %fusion.5 = f32[3,8,256]{2,1,0:T(8,128)S(1)} fusion(f32[1,5,3,256,256]{4,3,2,1,0:T(8,128)} %param.8, f32[3,8,256]{2,1,0:T(8,128)S(1)} %gather_fusion.2, pred[3]{0:T(512)(128)(4,1)S(1)} %compare_and_fusion.2), kind=kOutput, calls=%fused_computation.15 | convolution fusion | flops 18880512 | bytes 835587 | tf_op jit(solution)/shard_map/ist,stu->isu/dot_general | solution.py:47
  29.6 0.7 compare_convert_fusion
  30.8 1.6 %fusion.7 = f32[3,8,256]{2,1,0:T(8,128)S(1)} fusion(f32[1,5,3,256,256]{4,3,2,1,0:T(8,128)} %param.8, f32[3,8,256]{2,1,0:T(8,128)S(1)} %gather_fusion.1, pred[3]{0:T(512)(128)(4,1)S(1)} %compare_and_fusion.3), kind=kOutput, calls=%fused_computation.17 | convolution fusion | flops 18880512 | bytes 835587 | tf_op jit(solution)/shard_map/ist,stu->isu/dot_general | solution.py:47
  33.0 4.8 %collective-permute-start.1 = (f32[8,2048]{1,0:T(8,128)S(1)}, f32[8,2048]{1,0:T(8,128)S(1)}, u32[]{:S(2)}, u32[]{:S(2)}) collective-permute-start(f32[8,2048]{1,0:T(8,128)S(1)} %collective-permute-done), channel_id=1, source_target_pairs={{0,4},{4,8},{8,12},{12,16},{16,20},{20,24},{24,28},{1,5},{5,9},{9,... | collective-permute-start | bytes 196616 | tf_op jit(solution)/shard_map/ppermute | solution.py:16
  37.8 1.6 %fusion.3 = f32[3,8,256]{2,1,0:T(8,128)S(1)} fusion(f32[1,5,3,256,256]{4,3,2,1,0:T(8,128)} %param.8, f32[3,8,256]{2,1,0:T(8,128)S(1)} %gather_fusion.3, pred[3]{0:T(512)(128)(4,1)S(1)} %compare_and_fusion.1), kind=kOutput, calls=%fused_computation.13 | convolution fusion | flops 18880512 | bytes 835587 | tf_op jit(solution)/shard_map/ist,stu->isu/dot_general | solution.py:47
  39.4 1.3 %collective-permute-start.3 = (f32[8,2048]{1,0:T(8,128)S(1)}, f32[8,2048]{1,0:T(8,128)S(1)}, u32[]{:S(2)}, u32[]{:S(2)}) collective-permute-start(f32[8,2048]{1,0:T(8,128)S(1)} %collective-permute-done.2), channel_id=1, source_target_pairs={{4,0},{8,4},{12,8},{16,12},{20,16},{24,20},{28,24},{5,1},{9,5},{13... | collective-permute-start | bytes 196616 | tf_op jit(solution)/shard_map/ppermute | solution.py:16
  41.3 1.6 %fusion.9 = f32[3,8,256]{2,1,0:T(8,128)S(1)} fusion(f32[1,5,3,256,256]{4,3,2,1,0:T(8,128)} %param.8, f32[3,8,256]{2,1,0:T(8,128)S(1)} %gather_fusion, pred[3]{0:T(512)(128)(4,1)S(1)} %compare_and_fusion.4), kind=kOutput, calls=%fused_computation.19 | convolution fusion | flops 18880512 | bytes 835587 | tf_op jit(solution)/shard_map/ist,stu->isu/dot_general | solution.py:47
  42.9 0.9 %collective-permute-done.3 = f32[8,2048]{1,0:T(8,128)S(1)} collective-permute-done((f32[8,2048]{1,0:T(8,128)S(1)}, f32[8,2048]{1,0:T(8,128)S(1)}, u32[]{:S(2)}, u32[]{:S(2)}) %collective-permute-start.3) | collective-permute-done | bytes 65568 | tf_op jit(solution)/shard_map/ppermute | solution.py:16
  44.4 1.6 %fusion.1 = f32[3,8,256]{2,1,0:T(8,128)S(1)} fusion(f32[1,5,3,256,256]{4,3,2,1,0:T(8,128)} %param.8, f32[3,8,256]{2,1,0:T(8,128)S(1)} %gather_fusion.4, pred[3]{0:T(512)(128)(4,1)S(1)} %compare_and_fusion), kind=kOutput, calls=%fused_computation.11 | convolution fusion | flops 18880512 | bytes 835587 | tf_op jit(solution)/shard_map/ist,stu->isu/dot_general | solution.py:47
  48.3 1.0 %convolution_bitcast_fusion = f32[8,8]{0,1:T(8,128)S(1)} fusion(f32[8,2048]{1,0:T(8,128)} %bitcast.81, f32[8,2048]{1,0:T(8,128)S(1)} %all_gather.3), kind=kOutput, calls=%fused_computation.10 | convolution fusion | flops 1572864 | bytes 131328 | tf_op jit(solution)/shard_map/dot_general | solution.py:63
  49.4 9.1 %all-reduce.1 = (f32[8,8]{0,1:T(8,128)S(1)}, f32[8,8]{0,1:T(8,128)S(1)}) all-reduce(f32[8,8]{0,1:T(8,128)S(1)} %convolution_bitcast_fusion, f32[8,8]{0,1:T(8,128)S(1)} %fusion.83), channel_id=1, replica_groups=mesh['blk'=8,'help'=4] {'help'}, use_global_device_ids=true, to_apply=%region_1.3 | all-reduce | flops 128 | bytes 1024 | tf_op jit(solution)/shard_map/psum | solution.py:72
  58.5 15.5 %all-reduce = (f32[8,8]{0,1:T(8,128)S(1)}, f32[8,8]{0,1:T(8,128)S(1)}) all-reduce(f32[8,8]{0,1:T(8,128)S(1)} %get-tuple-element.22, f32[8,8]{0,1:T(8,128)S(1)} %get-tuple-element.23), channel_id=1, replica_groups=mesh['blk'=8,'help'=4] {'blk'}, use_global_device_ids=true, to_apply=%region_2.4 | all-reduce | flops 128 | bytes 1024 | tf_op jit(solution)/shard_map/psum | solution.py:71
  74.0 0.7 copy.12
  74.7 0.7 copy.13
  (34 shorter events, 5.8 us)
Async XLA Ops:
  7.2 68.2 %reduce-scatter.2.cloned.1.call-start = ((), (), s32[]{:S(2)}) async-start(), calls=%async_computation.1 | async-start | bytes 81920 | tf_op jit(solution)/shard_map/reduce_scatter | solution.py:74
  17.1 13.2 %collective-permute-start = (f32[8,2048]{1,0:T(8,128)S(1)}, f32[8,2048]{1,0:T(8,128)S(1)}, u32[]{:S(2)}, u32[]{:S(2)}) collective-permute-start(f32[8,2048]{1,0:T(8,128)S(1)} %all_gather.3), channel_id=1, source_target_pairs={{0,4},{4,8},{8,12},{12,16},{16,20},{20,24},{24,28},{1,5},{5,9},{9,... | collective-permute-start | bytes 196616 | tf_op jit(solution)/shard_map/ppermute | solution.py:16
  18.3 14.1 %collective-permute-start.2 = (f32[8,2048]{1,0:T(8,128)S(1)}, f32[8,2048]{1,0:T(8,128)S(1)}, u32[]{:S(2)}, u32[]{:S(2)}) collective-permute-start(f32[8,2048]{1,0:T(8,128)S(1)} %all_gather.3), channel_id=1, source_target_pairs={{4,0},{8,4},{12,8},{16,12},{20,16},{24,20},{28,24},{5,1},{9,5},{13... | collective-permute-start | bytes 196616 | tf_op jit(solution)/shard_map/ppermute | solution.py:16
  33.0 7.8 %collective-permute-start.1 = (f32[8,2048]{1,0:T(8,128)S(1)}, f32[8,2048]{1,0:T(8,128)S(1)}, u32[]{:S(2)}, u32[]{:S(2)}) collective-permute-start(f32[8,2048]{1,0:T(8,128)S(1)} %collective-permute-done), channel_id=1, source_target_pairs={{0,4},{4,8},{8,12},{12,16},{16,20},{20,24},{24,28},{1,5},{5,9},{9,... | collective-permute-start | bytes 196616 | tf_op jit(solution)/shard_map/ppermute | solution.py:16
  39.4 4.4 %collective-permute-start.3 = (f32[8,2048]{1,0:T(8,128)S(1)}, f32[8,2048]{1,0:T(8,128)S(1)}, u32[]{:S(2)}, u32[]{:S(2)}) collective-permute-start(f32[8,2048]{1,0:T(8,128)S(1)} %collective-permute-done.2), channel_id=1, source_target_pairs={{4,0},{8,4},{12,8},{16,12},{20,16},{24,20},{28,24},{5,1},{9,5},{13... | collective-permute-start | bytes 196616 | tf_op jit(solution)/shard_map/ppermute | solution.py:16
Sparse Core Ops, SparseCore 0:
  48.5 25.5 reduce-scatter.1
